TPU v7x, 256 devices: a whole 4x4x8 slice. The times are simulated.
256 devices in a mesh: row: 16 (over z, x_lo), col: 4 (over x_hi, core), layer: 4 (over y).
Axes of the slice: x: 4 (x_hi: 2, x_lo: 2; x = x_hi * 2 + x_lo), y: 4, z: 8, core: 2. Of those that a mesh axis runs over, the one named last changes fastest.
Arguments:
- density: bfloat16 [512, 16, 128, 128], P('row', 'col'), may hold values from -0.59765625 to 0.59765625
- block_offset: int32 [512, 16], P('row', 'col'), may hold values from 0 to 1, as said below
- filter_offset: int32 [64, 32], P('row', 'col'), may hold values from 0 to 3, as said below
- position: int32 [32], replicated, may hold values from 0 to 31, each once
Outputs:
- purified: float32 [64, 32, 128, 128], P(('row', 'layer'), 'col')
Inputs may be any that keep to these rules, and one draw needn't show every extreme that they name: `block_offset`: slots fall into groups of 1 consecutive slots; within each group of a block row the offsets rise strictly (a group of one slot holds a single offset). `filter_offset`: slots fall into groups of 2 consecutive slots; within each group of a row the offsets rise strictly (a group of one slot holds a single offset).
All inputs are finite; a program needn't handle non-finite values.
Results may differ from a plain program's by a relative error of at most 0.0027.
Values may be sent and summed in bfloat16 or wider, within the bound.
No kernel may reach another device: no remote copies, remote signals or barrier semaphores. Data moves between devices by JAX's collectives and lax.ppermute only.
A program may use at most 128 MiB of HBM per device.

v0:
```python
import jax
import jax.numpy as jnp
from jax import lax
from jax.sharding import PartitionSpec as P

W = 16
WF = 32
RA = 4


def from_behind(value, axis, steps):
    count = lax.axis_size(axis)
    pairs = [(source, (source + steps) % count) for source in range(count)]
    return lax.ppermute(value, axis, pairs)


def column_index(offsets, local_rows, position, image_of, slot_base, group_size):
    extent = position.shape[0]
    groups = (slot_base + jnp.arange(offsets.shape[1], dtype=jnp.int32)) // group_size * extent
    physical = (position[local_rows][:, None] + offsets) % extent
    return groups[None, :] + image_of[physical]


def block_multiply(left_blocks, local_rows, right_blocks, right_columns, targets):
    picked = right_blocks[local_rows]
    picked_columns = right_columns[local_rows]
    matches = picked_columns[:, :, None, :] == targets[:, None, :, None]
    chosen = jnp.einsum(
        "nsut,nstyz->nsuyz",
        matches.astype(jnp.bfloat16),
        picked,
        preferred_element_type=jnp.float32,
    ).astype(jnp.bfloat16)
    return jnp.einsum("nsxy,nsuyz->nuxz", left_blocks, chosen, preferred_element_type=jnp.float32)


def on_device(density, block_offset, filter_offset, position):
    rows_tile = density.shape[0]
    slots_tile = density.shape[1]
    edge = density.shape[2]
    row_count = lax.axis_size("row")
    layer_count = lax.axis_size("layer")
    group_block = W // row_count
    group_filter = WF // row_count
    filter_slots = filter_offset.shape[1]
    row_id = lax.axis_index("row")
    col_id = lax.axis_index("col")
    layer_id = lax.axis_index("layer")
    extent = position.shape[0]
    image_of = jnp.zeros((extent,), jnp.int32).at[position].set(jnp.arange(extent, dtype=jnp.int32))
    right_columns = column_index(
        block_offset,
        jnp.arange(rows_tile, dtype=jnp.int32),
        position,
        image_of,
        col_id * slots_tile,
        group_block,
    )
    target_columns = column_index(
        filter_offset,
        jnp.arange(RA, dtype=jnp.int32),
        position,
        image_of,
        col_id * filter_slots,
        group_filter,
    )
    share_rows = RA // layer_count
    step_count = row_count // layer_count
    carried = (density, right_columns)
    for bit_number in range(layer_count.bit_length() - 1):
        moved = from_behind((carried[0], carried[1]), "row", step_count * (1 << bit_number))
        taken = layer_id >> bit_number & 1 == 1
        carried = (jnp.where(taken, moved[0], carried[0]), jnp.where(taken, moved[1], carried[1]))
    panels = []
    for turn_index in range(step_count):
        if turn_index > 0:
            carried = from_behind((carried[0], carried[1]), "row", 1)
        source = (row_id - layer_id * step_count - turn_index) % row_count
        panels.append((source, carried))

    def gather_left(left_blocks, left_columns):
        return (
            lax.all_gather(left_blocks, "col", axis=1, tiled=True),
            lax.all_gather(left_columns, "col", axis=1, tiled=True),
        )

    def panel_product(left_blocks, left_columns, group_size):
        full_blocks, full_columns = gather_left(left_blocks, left_columns)
        running = jnp.zeros((RA, filter_slots, edge, edge), jnp.float32)
        for source, received in panels:
            start = source * group_size
            piece = lax.dynamic_slice_in_dim(full_blocks, start, group_size, 1)
            piece_columns = lax.dynamic_slice_in_dim(full_columns, start, group_size, 1)
            running = running + block_multiply(
                piece, piece_columns - source * rows_tile, received[0], received[1], target_columns
            )
        return running

    square = panel_product(density[:RA], right_columns[:RA], group_block)
    summed = lax.psum(square, "layer")
    square_own = lax.dynamic_slice_in_dim(summed, layer_id * share_rows, share_rows, 0)
    square_half = summed.astype(jnp.bfloat16)
    cube = panel_product(square_half, target_columns, group_filter)
    cube_own = lax.psum_scatter(cube, "layer", scatter_dimension=0, tiled=True)
    return 3.0 * square_own - 2.0 * cube_own


def solution(mesh):
    placed = (P("row", "col", None, None), P("row", "col"), P("row", "col"), P())
    return jax.shard_map(
        on_device,
        mesh=mesh,
        in_specs=placed,
        out_specs=P(("row", "layer"), "col", None, None),
        check_vma=False,
    )
```

profile of v0, /device:TPU:1, one launch (start us, length us, event | category | flops | bytes accessed | tf_op | source)
XLA Modules:
  0.0 888.2 jit_solution(15324507685565275466)
XLA Ops:
  6.5 3.8 collective-permute-start.2
  10.3 130.0 %collective-permute-done.2 = bf16[32,4,128,128]{3,2,1,0:T(8,128)(2,1)} collective-permute-done((bf16[32,4,128,128]{3,2,1,0:T(8,128)(2,1)}, bf16[32,4,128,128]{3,2,1,0:T(8,128)(2,1)}, u32[]{:S(2)}, u32[]{:S(2)}) %collective-permute-start.2) | collective-permute-done | bytes 4194336 | tf_op jit(solution)/shard_map/ppermute | solution.py:14
  140.3 4.6 broadcast_select_fusion
  144.9 58.2 %collective-permute-start.3 = (bf16[32,4,128,128]{3,2,1,0:T(8,128)(2,1)}, bf16[32,4,128,128]{3,2,1,0:T(8,128)(2,1)}, u32[]{:S(2)}, u32[]{:S(2)}) collective-permute-start(bf16[32,4,128,128]{3,2,1,0:T(8,128)(2,1)} %broadcast_select_fusion), channel_id=1, source_target_pairs={{0,128},{16,144},{32,160},{48,176},{64,192},{80,208},{96,224},{112... | collective-permute-start | bytes 12582920 | tf_op jit(solution)/shard_map/ppermute | solution.py:14
  203.1 180.2 %collective-permute-done.3 = bf16[32,4,128,128]{3,2,1,0:T(8,128)(2,1)} collective-permute-done((bf16[32,4,128,128]{3,2,1,0:T(8,128)(2,1)}, bf16[32,4,128,128]{3,2,1,0:T(8,128)(2,1)}, u32[]{:S(2)}, u32[]{:S(2)}) %collective-permute-start.3) | collective-permute-done | bytes 4194336 | tf_op jit(solution)/shard_map/ppermute | solution.py:14
  383.3 2.6 broadcast_select_fusion.1
  385.9 1.9 copy-done.3
  387.9 1.2 collective-permute-start.5
  389.1 92.5 %collective-permute-done.5 = bf16[32,4,128,128]{3,2,1,0:T(8,128)(2,1)} collective-permute-done((bf16[32,4,128,128]{3,2,1,0:T(8,128)(2,1)S(1)}, bf16[32,4,128,128]{3,2,1,0:T(8,128)(2,1)}, u32[]{:S(2)}, u32[]{:S(2)}) %collective-permute-start.5) | collective-permute-done | bytes 4194336 | tf_op jit(solution)/shard_map/ppermute | solution.py:14
  482.0 0.7 gather_fusion
  483.7 1.2 gather_fusion.1
  485.0 2.1 collective-permute-start
  487.2 1.9 slice.7
  490.0 92.1 %collective-permute-done.7 = bf16[32,4,128,128]{3,2,1,0:T(8,128)(2,1)} collective-permute-done((bf16[32,4,128,128]{3,2,1,0:T(8,128)(2,1)}, bf16[32,4,128,128]{3,2,1,0:T(8,128)(2,1)}, u32[]{:S(2)}, u32[]{:S(2)}) %collective-permute-start.7) | collective-permute-done | bytes 4194336 | tf_op jit(solution)/shard_map/ppermute | solution.py:14
  582.1 2.2 collective-permute-start.9
  585.2 94.4 %all-gather = s32[4,4,4]{2,1,0:T(4,128)S(1)} all-gather(s32[1,4,4]{2,1,0:T(4,128)S(1)} %bitcast.166), channel_id=1, replica_groups=mesh['row'=16,'col'=4,'layer'=4] {'col'}, dimensions={0}, use_global_device_ids=true | all-gather | bytes 320 | tf_op jit(solution)/shard_map/all_gather | solution.py:84
  680.4 5.3 collective-permute-start.1
  685.7 1.4 collective-permute-done.1
  687.1 4.7 collective-permute-done.4
  691.8 4.7 collective-permute-done.6
  698.2 3.0 collective-permute-done.8
  701.8 2.8 gather_fusion.5
  705.3 1.4 fusion.20
  706.7 2.8 gather_fusion.7
  710.2 2.8 fusion.18
  713.0 2.8 gather_fusion.9
  716.5 2.8 fusion.16
  719.2 2.8 gather_fusion.11
  722.7 4.2 add_bitcast_fusion
  727.0 66.7 %all-reduce.2.cloned.1.call-done = f32[4,8,128,128]{2,3,1,0:T(8,128)} async-done(((f32[4,8,128,128]{2,3,1,0:T(8,128)}), f32[4,8,128,128]{2,3,1,0:T(8,128)}) %all-reduce.2.cloned.1.call-update) | async-done | bytes 2097168 | tf_op jit(solution)/shard_map/psum | solution.py:100
  793.7 2.7 convert_element_type.44
  796.6 7.6 all-gather.1
  806.9 3.3 gather_fusion.13
  810.3 2.2 convolution_convert_fusion.3
  812.5 2.9 gather_fusion.15
  815.4 1.2 convolution_convert_fusion.2
  816.7 3.0 gather_fusion.17
  819.6 2.2 convolution_convert_fusion.1
  821.9 3.0 gather_fusion.19
  824.9 2.2 convolution_convert_fusion
  827.1 10.9 %all-gather.7.cloned.1.call-done = bf16[4,32,128,128]{2,3,1,0:T(8,128)(2,1)} async-done(((bf16[4,8,128,128]{2,3,1,0:T(8,128)(2,1)}), bf16[4,32,128,128]{2,3,1,0:T(8,128)(2,1)}) %all-gather.7.cloned.1.call-update) | async-done | bytes 4194320 | tf_op jit(solution)/shard_map/all_gather | solution.py:83
  838.0 2.7 fusion.1
  840.7 1.9 fusion.3
  842.6 2.0 fusion.5
  844.6 3.3 fusion
  848.0 31.4 %reduce-scatter.2.cloned.1.call-done = f32[1,8,128,128]{2,3,1,0:T(8,128)} async-done(((f32[4,8,128,128]{2,3,1,0:T(8,128)}), f32[1,8,128,128]{2,3,1,0:T(8,128)}) %reduce-scatter.2.cloned.1.call-update) | async-done | bytes 524304 | tf_op jit(solution)/shard_map/reduce_scatter | solution.py:104
  879.4 1.3 multiply_subtract_fusion
  880.7 1.0 copy.47
  (91 shorter events, 11.6 us)
Async XLA Ops:
  6.5 698.7 %all-gather.5.cloned.1.call-start = ((), (), s32[]{:S(2)}) async-start(), calls=%async_computation.1 | async-start | bytes 2621440 | tf_op jit(solution)/shard_map/all_gather | solution.py:83
  6.5 133.8 %collective-permute-start.2 = (bf16[32,4,128,128]{3,2,1,0:T(8,128)(2,1)}, bf16[32,4,128,128]{3,2,1,0:T(8,128)(2,1)}, u32[]{:S(2)}, u32[]{:S(2)}) collective-permute-start(bf16[32,4,128,128]{3,2,1,0:T(8,128)(2,1)} %param.4), channel_id=1, source_target_pairs={{0,64},{16,80},{32,96},{48,112},{64,128},{80,144},{96,160},{112,17... | collective-permute-start | bytes 12582920 | tf_op jit(solution)/shard_map/ppermute | solution.py:14
  144.9 238.4 %collective-permute-start.3 = (bf16[32,4,128,128]{3,2,1,0:T(8,128)(2,1)}, bf16[32,4,128,128]{3,2,1,0:T(8,128)(2,1)}, u32[]{:S(2)}, u32[]{:S(2)}) collective-permute-start(bf16[32,4,128,128]{3,2,1,0:T(8,128)(2,1)} %broadcast_select_fusion), channel_id=1, source_target_pairs={{0,128},{16,144},{32,160},{48,176},{64,192},{80,208},{96,224},{112... | collective-permute-start | bytes 12582920 | tf_op jit(solution)/shard_map/ppermute | solution.py:14
  203.1 278.9 %copy-start = (s32[32]{0:T(128)S(1)}, s32[32]{0:T(128)}, u32[]{:S(2)}) copy-start(s32[32]{0:T(128)} %param.7) | copy-start | bytes 388
  203.1 279.6 %copy-start.4 = (s32[32,4]{0,1:T(4,128)S(1)}, s32[32,4]{0,1:T(4,128)}, u32[]{:S(2)}) copy-start(s32[32,4]{0,1:T(4,128)} %param.5) | copy-start | bytes 1540
  385.9 2.0 copy-start.3
  387.9 93.8 %collective-permute-start.5 = (bf16[32,4,128,128]{3,2,1,0:T(8,128)(2,1)S(1)}, bf16[32,4,128,128]{3,2,1,0:T(8,128)(2,1)}, u32[]{:S(2)}, u32[]{:S(2)}) collective-permute-start(bf16[32,4,128,128]{3,2,1,0:T(8,128)(2,1)S(1)} %broadcast_select_fusion.1), channel_id=1, source_target_pairs={{0,16},{16,32},{32,48},{48,64},{64,80},{80,96},{96,112},{112,128},... | collective-permute-start | bytes 12582920 | tf_op jit(solution)/shard_map/ppermute | solution.py:14
  481.6 100.5 %collective-permute-start.7 = (bf16[32,4,128,128]{3,2,1,0:T(8,128)(2,1)}, bf16[32,4,128,128]{3,2,1,0:T(8,128)(2,1)}, u32[]{:S(2)}, u32[]{:S(2)}) collective-permute-start(bf16[32,4,128,128]{3,2,1,0:T(8,128)(2,1)} %collective-permute-done.5), channel_id=1, source_target_pairs={{0,16},{16,32},{32,48},{48,64},{64,80},{80,96},{96,112},{112,128},... | collective-permute-start | bytes 12582920 | tf_op jit(solution)/shard_map/ppermute | solution.py:14
  484.9 4.9 copy-start.5
  485.0 195.3 %collective-permute-start = (s32[32,4]{1,0:T(8,128)S(1)}, s32[32,4]{1,0:T(8,128)S(1)}, u32[]{:S(2)}, u32[]{:S(2)}) collective-permute-start(s32[32,4]{1,0:T(8,128)S(1)} %broadcast_add_fusion), channel_id=1, source_target_pairs={{0,64},{16,80},{32,96},{48,112},{64,128},{80,144},{96,160},{112,17... | collective-permute-start | bytes 1544 | tf_op jit(solution)/shard_map/ppermute | solution.py:14
  489.1 304.6 %all-reduce.2.cloned.1.call-start = ((), (), s32[]{:S(2)}) async-start(), calls=%async_computation.2 | async-start | bytes 4194304 | tf_op jit(solution)/shard_map/psum | solution.py:100
  582.1 137.1 %collective-permute-start.9 = (bf16[32,4,128,128]{3,2,1,0:T(8,128)(2,1)}, bf16[32,4,128,128]{3,2,1,0:T(8,128)(2,1)}, u32[]{:S(2)}, u32[]{:S(2)}) collective-permute-start(bf16[32,4,128,128]{3,2,1,0:T(8,128)(2,1)} %collective-permute-done.7), channel_id=1, source_target_pairs={{0,16},{16,32},{32,48},{48,64},{64,80},{80,96},{96,112},{112,128},... | collective-permute-start | bytes 12582920 | tf_op jit(solution)/shard_map/ppermute | solution.py:14
  680.4 6.7 collective-permute-start.1
  687.1 4.7 collective-permute-start.4
  691.8 4.7 collective-permute-start.6
  696.5 4.7 collective-permute-start.8
  727.0 111.1 %all-gather.7.cloned.1.call-start = ((), (), s32[]{:S(2)}) async-start(), calls=%async_computation.3 | async-start | bytes 5242880 | tf_op jit(solution)/shard_map/all_gather | solution.py:83
  796.5 82.9 %reduce-scatter.2.cloned.1.call-start = ((), (), s32[]{:S(2)}) async-start(), calls=%async_computation.4 | async-start | bytes 2621440 | tf_op jit(solution)/shard_map/reduce_scatter | solution.py:104
  838.0 2.7 copy-start.1
  842.6 2.0 copy-start.2
Sparse Core Ops, SparseCore 0:
  489.2 41.7 all-gather.4
  727.1 66.5 all-reduce.1
  796.6 41.3 all-gather.6
  848.1 31.2 reduce-scatter.1
where the time goes:
time: 889 us; the launch traced here: 888 us
  waiting for transfers between devices  618 us (70%)
  blocking collectives  102 us (11%)
  starting transfers between devices  73.4 us (8%)
  local copies, waits for them, and re-layouts  38.1 us (4%)
  matrix products  31.5 us (4%)
  between operations  13.6 us (2%)
  other arithmetic  11.8 us (1%)
    ppermute x10, waiting for transfers between devices, from_behind(): return lax.ppermute(value, axis, pairs)  509 us
    all_gather x2, blocking collectives, gather_left(): lax.all_gather(left_columns, 'col', axis=1, tiled=True)  102 us
    ppermute x10, starting transfers between devices, from_behind(): return lax.ppermute(value, axis, pairs)  73.2 us
    psum x1, waiting for transfers between devices, on_device(): summed = lax.psum(square, 'layer')  66.7 us
    reduce_scatter x1, waiting for transfers between devices, on_device(): cube_own = lax.psum_scatter(cube, 'layer', scatter_dimension=0, tiled=True)  31.4 us
    gather x8, local copies, waits for them, and re-layouts, block_multiply(): picked = right_blocks[local_rows]  23.5 us
    dot_general x8, matrix products, block_multiply(): jnp.einsum('nsxy,nsuyz->nuxz', left_blocks, chosen, preferred_element_typ...  21.1 us
  transfers between devices with their start and end apart: 14, of which 11 were waited for; matrix products, arithmetic and copies ran while one was open for 6% of the time, Pallas kernels for 0%

commit v1 on v0

v1 whole, which is shorter than its diff:
```python
import jax
import jax.numpy as jnp
from jax import lax
from jax.sharding import PartitionSpec as P

CANDIDATES = 4


def on_device(density, block_offset, filter_offset, position):
    extent = position.shape[0]
    slots_tile = density.shape[1]
    col_id = lax.axis_index("col")
    layer_id = lax.axis_index("layer")
    image_of = jnp.zeros((extent,), jnp.int32).at[position].set(jnp.arange(extent, dtype=jnp.int32))
    base = position[layer_id]
    ks = jnp.arange(CANDIDATES, dtype=jnp.int32)
    cand = image_of[(base + ks) % extent]

    picked = density[cand]
    picked_offsets = block_offset[cand]
    gathered = lax.all_gather(picked, "row", axis=0, tiled=False)
    gathered_offsets = lax.all_gather(picked_offsets, "row", axis=0, tiled=False)

    left = lax.all_gather(density[layer_id], "col", axis=0, tiled=True)
    own_ints = jnp.concatenate([block_offset[layer_id], filter_offset[layer_id]])
    all_ints = lax.all_gather(own_ints, "col", axis=0, tiled=False)
    left_offsets = all_ints[:, :slots_tile].reshape(-1)
    filter_all = all_ints[:, slots_tile:].reshape(-1)

    t_count = slots_tile
    groups = col_id * slots_tile + jnp.arange(t_count, dtype=jnp.int32)
    filter_own = filter_offset[layer_id].reshape(t_count, -1)
    target = groups[:, None] * extent + image_of[(base + filter_own) % extent]

    def right_columns(w_index, k_index):
        offsets = gathered_offsets[w_index, k_index]
        physical = (position[cand[k_index]][:, None] + offsets) % extent
        return groups[None, :] * extent + image_of[physical]

    row_groups = left.shape[0]
    w_all = jnp.arange(row_groups, dtype=jnp.int32)
    square_k = left_offsets
    square_right = gathered[w_all, square_k]
    square_match = right_columns(w_all, square_k)[:, :, None] == target[None, :, :]
    square_parts = jnp.einsum("wxy,wtyz->wtxz", left, square_right, preferred_element_type=jnp.float32)
    square = jnp.sum(
        jnp.where(square_match[:, :, :, None, None], square_parts[:, :, None], 0.0), axis=0
    )

    square_half = square.astype(jnp.bfloat16).reshape(-1, *square.shape[2:])
    square_all = lax.all_gather(square_half, "col", axis=0, tiled=True)

    v_all = jnp.arange(square_all.shape[0], dtype=jnp.int32)
    cube_w = v_all // (square_all.shape[0] // row_groups)
    cube_right = gathered[cube_w, filter_all]
    cube_match = right_columns(cube_w, filter_all)[:, :, None] == target[None, :, :]
    cube_parts = jnp.einsum("vxy,vtyz->vtxz", square_all, cube_right, preferred_element_type=jnp.float32)
    cube = jnp.sum(jnp.where(cube_match[:, :, :, None, None], cube_parts[:, :, None], 0.0), axis=0)

    result = 3.0 * square - 2.0 * cube
    return result.reshape(1, -1, *result.shape[2:])


def solution(mesh):
    placed = (P("row", "col", None, None), P("row", "col"), P("row", "col"), P())
    return jax.shard_map(
        on_device,
        mesh=mesh,
        in_specs=placed,
        out_specs=P(("row", "layer"), "col", None, None),
        check_vma=False,
    )
```

time: 889 us -> 274 us (0.31)
  waiting for transfers between devices: 618 us -> 130 us
  starting transfers between devices: 73.4 us -> 0.04 us
  blocking collectives: 102 us -> 60.6 us
  matrix products: 31.5 us -> 9.78 us
    ppermute x10 -> x0, waiting for transfers between devices: 509 us -> none  [from_behind(): return lax.ppermute(value, axis, pairs)]
    all_gather x2, waiting for transfers between devices: 10.9 us -> 130 us  [the longest x1 118 us: on_device(): gathered = lax.all_gather(picked, 'row', axis=0, tiled=False)]
    ppermute x10 -> x0, starting transfers between devices: 73.2 us -> none  [from_behind(): return lax.ppermute(value, axis, pairs)]
    psum x1 -> x0, waiting for transfers between devices: 66.7 us -> none  [on_device(): summed = lax.psum(square, 'layer')]
    all_gather x2, blocking collectives: 102 us -> 54 us  [the longest x1 32.3 us: on_device(): lax.all_gather(picked_offsets, 'row', axis=0, tiled=False)]
    reduce_scatter x1 -> x0, waiting for transfers between devices: 31.4 us -> none  [on_device(): cube_own = lax.psum_scatter(cube, 'layer', scatter_dimension=0, tiled=True)]
    dot_general x16 -> x2, matrix products: 31.5 us -> 9.78 us  [the longest x1 7.03 us: on_device(): jnp.einsum('vxy,vtyz->vtxz', square_all, cube_right, preferred_element_ty...]
    transpose x0 -> x2, local copies, waits for them, and re-layouts: none -> 14.3 us  [the longest x1 8.95 us: on_device(): jnp.einsum('vxy,vtyz->vtxz', square_all, cube_right, preferred_element_ty...]
  transfers between devices with their start and end apart: 14 -> 2, of which waited for: 11 -> 2; matrix products, arithmetic and copies ran while one was open for 6% -> 8% of each run, Pallas kernels for 0% -> 0%
where the time goes in v1:
time: 274 us; the launch traced here: 273 us
  waiting for transfers between devices  130 us (47%)
  blocking collectives  60.6 us (22%)
  local copies, waits for them, and re-layouts  43.5 us (16%)
  other arithmetic  14.5 us (5%)
  between operations  14.2 us (5%)
  matrix products  9.78 us (4%)
    all_gather x1, waiting for transfers between devices, on_device(): gathered = lax.all_gather(picked, 'row', axis=0, tiled=False)  118 us
    all_gather x1, blocking collectives, on_device(): lax.all_gather(picked_offsets, 'row', axis=0, tiled=False)  32.3 us
    all_gather x1, blocking collectives, on_device(): left = lax.all_gather(density[layer_id], 'col', axis=0, tiled=True)  21.7 us
    all_gather x1, waiting for transfers between devices, on_device(): square_all = lax.all_gather(square_half, 'col', axis=0, tiled=True)  12.1 us
    transpose x1, local copies, waits for them, and re-layouts, on_device(): jnp.einsum('vxy,vtyz->vtxz', square_all, cube_right, preferred_element_ty...  8.95 us
    dot_general x1, matrix products, on_device(): jnp.einsum('vxy,vtyz->vtxz', square_all, cube_right, preferred_element_ty...  7.03 us
    unnamed x1, blocking collectives  6.57 us
    gather x1, local copies, waits for them, and re-layouts, on_device(): cube_right = gathered[cube_w, filter_all]  6.44 us
  transfers between devices with their start and end apart: 2, of which 2 were waited for; matrix products, arithmetic and copies ran while one was open for 8% of the time, Pallas kernels for 0%

profile of v1, /device:TPU:1, one launch (start us, length us, event | category | flops | bytes accessed | tf_op | source)
XLA Modules:
  0.0 273.0 jit_solution(4245343860668164165)
XLA Ops:
  6.5 0.7 compare_select_fusion.10
  7.3 1.2 dynamic_slice.13
  8.5 0.6 fusion.10
  9.1 0.7 scatter_custom_fusion
  9.8 0.6 gather_fusion
  10.4 3.6 %gather_fusion.7 = bf16[4,4,128,128]{3,2,1,0:T(8,128)(2,1)} fusion(bf16[32,4,128,128]{3,2,1,0:T(8,128)(2,1)} %param.4, s32[1024]{0:T(1024)S(1)} %pad_clamp_fusion.4), kind=kCustom, calls=%fused_computation.7 | custom fusion | bytes 1048592 | tf_op jit(solution)/shard_map/gather | solution.py:19
  14.1 0.9 dynamic-slice_reduce_fusion
  15.0 0.8 copy.31
  15.7 1.3 dynamic-slice
  17.6 1.3 add_reduce_fusion
  18.9 0.2 add_dynamic-update-slice_fusion
  19.1 6.6 %all-reduce = s32[48]{0:T(128)S(1)} all-reduce(s32[48]{0:T(128)S(1)} %add_dynamic-update-slice_fusion), channel_id=2, replica_groups=mesh['row'=16,'col'=4,'layer'=4] {'col'}, use_global_device_ids=true, to_apply=%add | all-reduce | flops 48 | bytes 384
  25.7 0.1 reshape.482
  25.9 0.1 reshape.532
  26.0 0.6 gather_fusion.6
  26.8 0.7 gather_fusion.1
  27.5 0.7 gather_fusion.2
  28.1 0.6 gather_fusion.3
  28.7 32.3 %all-gather.4 = s32[16,4,4]{2,1,0:T(4,128)S(1)} all-gather(s32[1,4,4]{2,1,0:T(4,128)S(1)} %bitcast.73), channel_id=3, replica_groups=mesh['row'=16,'col'=4,'layer'=4] {'row'}, dimensions={0}, use_global_device_ids=true | all-gather | bytes 1088 | tf_op jit(solution)/shard_map/all_gather | solution.py:22
  61.0 0.6 gather_fusion.4
  61.7 0.1 copy.33
  61.8 0.1 reshape.524
  61.9 0.8 gather_fusion.5
  62.7 0.9 dynamic-slice_bitcast_fusion
  63.7 21.7 %all-gather.3 = bf16[1,16,128,128]{3,2,0,1:T(8,128)(2,1)S(1)} all-gather(bf16[1,4,128,128]{3,2,0,1:T(8,128)(2,1)S(1)} %dynamic-slice_bitcast_fusion), channel_id=5, replica_groups=mesh['row'=16,'col'=4,'layer'=4] {'col'}, dimensions={1}, use_global_device_ids=true | all-gather | bytes 655360 | tf_op jit(solution)/shard_map/all_gather | solution.py:24
  85.5 0.1 broadcast_compare_fusion.1
  85.6 118.2 %all-gather.10.cloned.1.call-done = bf16[64,4,128,128]{3,2,1,0:T(8,128)(2,1)} async-done(((bf16[4,4,128,128]{3,2,1,0:T(8,128)(2,1)}), bf16[64,4,128,128]{3,2,1,0:T(8,128)(2,1)}) %all-gather.10.cloned.1.call-update) | async-done | bytes 8388624 | tf_op jit(solution)/shard_map/all_gather | solution.py:21
  203.7 4.3 %gather_fusion.8 = bf16[16,4,128,128]{3,2,1,0:T(8,128)(2,1)S(1)} fusion(bf16[16,4,4,128,128]{4,3,2,1,0:T(8,128)(2,1)} %bitcast.69, s32[16]{0:T(128)S(1)} %get-tuple-element.14), kind=kCustom, calls=%fused_computation.8 | custom fusion | bytes 4194432 | tf_op jit(solution)/shard_map/gather | solution.py:43
  208.1 2.8 %convolution_bitcast_fusion.1 = f32[16,4,128,128]{2,3,1,0:T(8,128)} fusion(bf16[16,4,128,128]{3,2,1,0:T(8,128)(2,1)S(1)} %gather_fusion.8, bf16[1,16,128,128]{3,2,0,1:T(8,128)(2,1)S(1)} %all-gather.3), kind=kOutput, calls=%fused_computation.17 | convolution fusion | flops 268435456 | bytes 6815744 | tf_op jit(solution)/shard_map/wxy,wtyz->wtxz/dot_general | solution.py:45
  210.8 5.4 %copy.36 = f32[16,4,128,128]{3,2,1,0:T(8,128)} copy(f32[16,4,128,128]{2,3,1,0:T(8,128)} %convolution_bitcast_fusion.1) | data formatting | bytes 8388608 | tf_op jit(solution)/shard_map/wxy,wtyz->wtxz/transpose | solution.py:45
  216.2 2.7 select_reduce_fusion.1
  218.9 0.7 convert_element_type.7
  219.7 0.1 reshape.483
  219.8 0.6 fusion.18
  220.4 2.4 fusion.13
  222.8 0.7 gather_fusion.9
  223.5 0.7 gather_fusion.10
  224.3 0.1 copy.38
  224.4 0.1 reshape.579
  224.5 1.2 gather_fusion.11
  225.7 0.1 reshape.578
  225.8 0.1 broadcast_compare_fusion
  225.9 6.4 %gather_fusion.12 = bf16[32,4,128,128]{3,2,1,0:T(8,128)(2,1)} fusion(bf16[16,4,4,128,128]{4,3,2,1,0:T(8,128)(2,1)} %bitcast.70, s32[32]{0:T(128)S(1)} %get-tuple-element.8), kind=kCustom, calls=%fused_computation.12 | custom fusion | bytes 8388864 | tf_op jit(solution)/shard_map/gather | solution.py:55
  232.4 12.1 %all-gather.8.cloned.1.call-done = bf16[32,128,128]{2,1,0:T(8,128)(2,1)} async-done(((bf16[8,128,128]{2,1,0:T(8,128)(2,1)}), bf16[32,128,128]{2,1,0:T(8,128)(2,1)}) %all-gather.8.cloned.1.call-update) | async-done | bytes 1048592 | tf_op jit(solution)/shard_map/all_gather | solution.py:51
  244.5 7.0 %convolution_bitcast_fusion = f32[32,4,128,128]{2,3,1,0:T(8,128)} fusion(bf16[32,4,128,128]{3,2,1,0:T(8,128)(2,1)} %gather_fusion.12, bf16[32,128,128]{2,1,0:T(8,128)(2,1)} %all-gather.8.cloned.1.call-done), kind=kOutput, calls=%fused_computation.16 | convolution fusion | flops 536870912 | bytes 13631488 | tf_op jit(solution)/shard_map/vxy,vtyz->vtxz/dot_general | solution.py:57
  251.5 9.0 %copy.40 = f32[32,4,128,128]{3,2,1,0:T(8,128)} copy(f32[32,4,128,128]{2,3,1,0:T(8,128)} %convolution_bitcast_fusion) | data formatting | bytes 16777216 | tf_op jit(solution)/shard_map/vxy,vtyz->vtxz/transpose | solution.py:57
  260.5 4.7 %select_reduce_fusion = f32[4,2,128,128]{3,2,1,0:T(8,128)S(1)} fusion(f32[32,4,128,128]{3,2,1,0:T(8,128)} %copy.40, pred[32,4,2]{2,1,0:T(4,128)(4,1)S(1)} %broadcast_compare_fusion), kind=kLoop, calls=%fused_computation.14 | loop fusion | flops 8257536 | bytes 8913152 | tf_op jit(solution)/shard_map/reduce_sum | solution.py:58
  265.2 0.9 multiply_subtract_fusion
  (33 shorter events, 0.9 us)
Async XLA Ops:
  6.5 20.9 %copy-start = (s32[32]{0:T(128)S(1)}, s32[32]{0:T(128)}, u32[]{:S(2)}) copy-start(s32[32]{0:T(128)} %param.7) | copy-start | bytes 388
  6.5 197.2 %all-gather.10.cloned.1.call-start = ((), (), s32[]{:S(2)}) async-start(), calls=%async_computation.1 | async-start | bytes 8912896 | tf_op jit(solution)/shard_map/all_gather | solution.py:21
  14.0 230.5 %all-gather.8.cloned.1.call-start = ((), (), s32[]{:S(2)}) async-start(), calls=%async_computation | async-start | bytes 1310720 | tf_op jit(solution)/shard_map/all_gather | solution.py:51
Sparse Core Ops, SparseCore 0:
  14.2 189.5 all-gather.9
  219.8 24.7 all-gather.7
